TPU v7x, 128 devices: a whole 4x4x4 slice. The times are simulated.
128 devices in a mesh: row: 16 (over z, x), col: 8 (over y, core).
Axes of the slice: x: 4, y: 4, z: 4, core: 2. Of those that a mesh axis runs over, the one named last changes fastest.
Arguments:
- psi: bfloat16 [2048, 16, 1024], P('row', None, 'col'), may hold values from -6 to 6
- env_left: bfloat16 [16, 3, 128, 128, 34], P('row'), may hold values from -0.0546875 to 0.0546875
- env_right: bfloat16 [8, 3, 128, 34, 128], P('col'), may hold values from -0.3125 to 0.3125
- first_site_operator: bfloat16 [34, 34, 4, 4], replicated, may hold values from -0.5 to 0.5
- mpo_right: bfloat16 [34, 34, 4, 4], replicated, may hold values from -0.5 to 0.5
- block_mask: int32 [16, 8], P('row', 'col'), may hold values 0 or 1
- left_live: int32 [16], P('row'), may hold values from 64 to 128, as said below
- right_live: int32 [8], P('col'), may hold values from 64 to 128, as said below
Outputs:
- hpsi: bfloat16 [2048, 16, 1024], P('row', None, 'col')
- residual: bfloat16 [2048, 16, 1024], P('row', None, 'col')
- quotient: float32 [], replicated
Inputs may be any that keep to these rules, and one draw needn't show every extreme that they name: `left_live`: a block is either full or is the last block of a sector with fewer live states; some block is full. `right_live`: a block is either full or is the last block of a sector with fewer live states; some block is full.
All inputs are finite; a program needn't handle non-finite values. No bound on the sum of `block_mask` on one device may be relied on, other than what follows from the above.
Results may differ from a plain program's by a relative error of at most 0.0064.
Values may be sent and summed in bfloat16 or wider, within the bound.
No kernel may reach another device: no remote copies, remote signals or barrier semaphores. Data moves between devices by JAX's collectives and lax.ppermute only.
A program may use at most 192 MiB of HBM per device.

v0:
```python
import jax
import jax.numpy as jnp
from jax import lax
from jax.sharding import PartitionSpec as P


def padded(block, sides, width):
    for axis, dim in sides:
        count = lax.axis_size(axis)
        forward = [(i, i + 1) for i in range(count - 1)]
        backward = [(target, source) for source, target in forward]
        low = lax.ppermute(
            lax.slice_in_dim(block, block.shape[dim] - width, None, axis=dim), axis, forward
        )
        high = lax.ppermute(lax.slice_in_dim(block, 0, width, axis=dim), axis, backward)
        block = jnp.concatenate([low, block, high], axis=dim)
    return block


def from_behind(block, axis, distance):
    devices = range(lax.axis_size(axis))
    route = [(i - distance, i) for i in devices if i - distance in devices]
    return lax.ppermute(block, axis, route)


def live_pattern(block_mask, left_live, right_live, block_rows):
    inside = lax.broadcasted_iota(jnp.int32, (block_rows,), 0)
    row_ok = (inside[None, :] < left_live[:, None]).reshape(-1)
    col_ok = (inside[None, :] < right_live[:, None]).reshape(-1)
    expanded = jnp.repeat(jnp.repeat(block_mask, block_rows, axis=0), block_rows, axis=1)
    return (expanded > 0) & row_ok[:, None] & col_ok[None, :]


def on_device(
    psi, env_left, env_right, first_site_operator, mpo_right, block_mask, left_live, right_live
):
    blocks = env_left.shape[0]
    block_rows = env_left.shape[2]
    mpo_width = env_left.shape[4]
    states = psi.shape[1]
    site_states = first_site_operator.shape[2]
    live_mask = live_pattern(block_mask, left_live, right_live, block_rows)
    masked_wavefunction = psi * live_mask[:, None, :].astype(jnp.bfloat16)
    widened = padded(masked_wavefunction, (("col", 2),), block_rows)
    right_matrix = env_right[0].reshape(3 * block_rows, mpo_width * block_rows)
    strip = widened.reshape(block_rows * states, 3 * block_rows)
    section_one = jnp.dot(strip, right_matrix, preferred_element_type=jnp.float32).astype(
        jnp.bfloat16
    )
    section_one = section_one.reshape(block_rows, site_states, site_states, mpo_width, block_rows)
    second_section = jnp.einsum(
        "mnts,xasnb->xamtb", mpo_right, section_one, preferred_element_type=jnp.float32
    ).astype(jnp.bfloat16)
    third_section = jnp.einsum(
        "dquo,woqzj->wduzj", first_site_operator, second_section, preferred_element_type=jnp.float32
    ).astype(jnp.bfloat16)
    outcomes = [third_section.reshape(block_rows * mpo_width, states * block_rows)]

    def couple_left(coupling, operand):
        return jnp.dot(
            coupling.reshape(block_rows, block_rows * mpo_width),
            operand,
            preferred_element_type=jnp.float32,
        )

    running = couple_left(env_left[0, 1], outcomes[0])
    totals = [running]
    from_prev = from_behind(outcomes[blocks - 1], "row", 1)
    from_next = from_behind(outcomes[0], "row", -1)
    totals[0] = totals[0] + couple_left(env_left[0, 0], from_prev)
    totals[blocks - 1] = totals[blocks - 1] + couple_left(env_left[blocks - 1, 2], from_next)
    hamiltonian_times_wavefunction = jnp.stack(totals).reshape(
        blocks * block_rows, states, block_rows
    )
    live_float = live_mask[:, None, :].astype(jnp.float32)
    applied = hamiltonian_times_wavefunction * live_float
    psi_float = masked_wavefunction.astype(jnp.float32)
    numerator, denominator = lax.psum(
        (jnp.sum(psi_float * applied), jnp.sum(psi_float * psi_float)), ("row", "col")
    )
    quotient = numerator / (denominator + 1e-06)
    return (
        applied.astype(jnp.bfloat16),
        (applied - quotient * psi_float).astype(jnp.bfloat16),
        quotient,
    )


def solution(mesh):
    return jax.shard_map(
        on_device,
        mesh=mesh,
        in_specs=(
            P("row", None, "col"),
            P("row", None, None, None, None),
            P("col", None, None, None, None),
            P(),
            P(),
            P("row", "col"),
            P("row"),
            P("col"),
        ),
        out_specs=(P("row", None, "col"), P("row", None, "col"), P()),
        check_vma=False,
    )
```

profile of v0, /device:TPU:1, one launch (start us, length us, event | category | flops | bytes accessed | tf_op | source)
XLA Modules:
  0.0 630.1 jit_solution(1653721309837381646)
XLA Ops:
  0.6 0.0 copy-start
  2.6 0.1 and_convert_fusion
  2.7 1.1 broadcast_multiply_fusion
  3.8 4.6 collective-permute-start
  8.4 1.9 collective-permute-start.1
  10.4 4.2 copy.13
  14.5 0.0 collective-permute-done
  14.5 4.4 collective-permute-done.1
  18.9 0.2 pad_maximum_fusion
  19.2 12.6 %convolution_convert_fusion = bf16[2048,4352]{1,0:T(8,128)(2,1)} fusion(bf16[2048,384]{1,0:T(8,128)(2,1)S(1)} %bitcast.74, bf16[48,8,34,128]{3,2,1,0:T(8,128)(2,1)S(1)} %bitcast.73), kind=kOutput, calls=%fused_computation.7 | convolution fusion | flops 6854017024 | bytes 22740992 | tf_op jit(solution)/shard_map/dot_general | solution.py:47
  31.7 29.7 %reshape.85 = bf16[128,4,4,34,128,1]{4,3,2,1,0,5:T(8,128)(2,1)} reshape(bf16[2048,4352]{1,0:T(8,128)(2,1)} %convolution_convert_fusion) | data formatting | bytes 35651584 | tf_op jit(solution)/shard_map/reshape | solution.py:50
  61.4 0.0 copy-done
  61.4 0.0 copy-start.4
  61.4 21.4 %fusion.39 = bf16[128,4,34,4,128,1]{4,2,1,5,3,0:T(8,128)(2,1)} fusion(bf16[128,4,4,34,128,1]{4,3,2,1,0,5:T(8,128)(2,1)} %reshape.85, bf16[34,34,4,4,1,1]{1,3,2,0,4,5:T(4,128)(2,1)S(1)} %bitcast.72), kind=kOutput, calls=%fused_computation.2.clone.clone.clone.clone.1 | convolution fusion | flops 2433220608 | bytes 35688576 | tf_op jit(solution)/shard_map/mnts,xasnb->xamtb/dot_general | solution.py:51
  82.8 0.0 copy-done.4
  82.8 21.3 %fusion.3 = bf16[128,34,4,4,128]{4,1,2,3,0:T(8,128)(2,1)} fusion(bf16[34,34,4,4,1,1]{1,3,2,0,5,4:T(4,128)(2,1)S(1)} %bitcast.76, bf16[128,4,34,4,128,1]{4,2,1,5,3,0:T(8,128)(2,1)} %fusion.39), kind=kOutput, calls=%fused_computation.4 | convolution fusion | flops 2433220608 | bytes 35688576 | tf_op jit(solution)/shard_map/dquo,woqzj->wduzj/dot_general | solution.py:54
  104.1 17.6 %copy.15 = bf16[128,34,4,4,128]{4,3,2,1,0:T(4,128)(2,1)} copy(bf16[128,34,4,4,128]{4,1,2,3,0:T(8,128)(2,1)} %fusion.3) | data formatting | bytes 35651584 | tf_op jit(solution)/shard_map/convert_element_type | solution.py:56
  121.7 29.3 %reshape.84 = bf16[4352,2048]{1,0:T(8,128)(2,1)} reshape(bf16[128,34,4,4,128]{4,3,2,1,0:T(4,128)(2,1)} %copy.15) | data formatting | bytes 35651584 | tf_op jit(solution)/shard_map/reshape | solution.py:57
  151.0 9.3 %collective-permute-start.2 = (bf16[4352,2048]{1,0:T(8,128)(2,1)}, bf16[4352,2048]{1,0:T(8,128)(2,1)}, u32[]{:S(2)}, u32[]{:S(2)}) collective-permute-start(bf16[4352,2048]{1,0:T(8,128)(2,1)} %reshape.84), channel_id=1, source_target_pairs={{0,8},{8,16},{16,24},{24,32},{32,40},{40,48},{48,56},{56,64},{64,7... | collective-permute-start | bytes 53477384 | tf_op jit(solution)/shard_map/ppermute | solution.py:23
  160.3 1.3 collective-permute-start.3
  161.6 3.7 fusion.21
  165.3 2.1 copy.16
  167.4 1.2 reshape_squeeze.13
  168.6 2.1 copy.17
  170.8 1.2 reshape_squeeze.14
  172.0 1.4 copy.18
  173.4 0.4 reshape_squeeze.15
  173.8 0.0 copy-start.3
  173.8 9.0 %fusion.22 = f32[2048,128]{1,0:T(8,128)S(1)} fusion(bf16[4352,2048]{1,0:T(8,128)(2,1)} %reshape.84, bf16[128,4352]{0,1:T(8,128)(2,1)} %reshape_squeeze.13), kind=kOutput, calls=%fused_computation.29 | convolution fusion | flops 2281701376 | bytes 19988480 | tf_op jit(solution)/shard_map/dot_general | solution.py:60
  182.8 348.3 %collective-permute-done.2 = bf16[4352,2048]{1,0:T(8,128)(2,1)} collective-permute-done((bf16[4352,2048]{1,0:T(8,128)(2,1)}, bf16[4352,2048]{1,0:T(8,128)(2,1)}, u32[]{:S(2)}, u32[]{:S(2)}) %collective-permute-start.2) | collective-permute-done | bytes 17825824 | tf_op jit(solution)/shard_map/ppermute | solution.py:23
  531.1 0.0 copy-done.3
  531.1 8.9 %convolution_add_fusion.1 = f32[2048,128]{1,0:T(8,128)S(1)} fusion(f32[2048,128]{1,0:T(8,128)S(1)} %fusion.22, bf16[4352,2048]{1,0:T(8,128)(2,1)} %collective-permute-done.2, bf16[128,4352]{0,1:T(8,128)(2,1)S(1)} %copy-done.3), kind=kOutput, calls=%fused_computation.11 | convolution fusion | flops 2281963520 | bytes 21037056 | tf_op jit(solution)/shard_map/dot_general | solution.py:60
  540.0 0.0 copy-start.2
  540.0 1.4 collective-permute-done.3
  541.3 0.0 copy-start.1
  541.3 9.8 %convolution_add_fusion = f32[2048,128]{1,0:T(8,128)} fusion(f32[2048,128]{1,0:T(8,128)S(1)} %convolution_add_fusion.1, bf16[4352,2048]{1,0:T(8,128)(2,1)} %collective-permute-done.3, bf16[128,4352]{0,1:T(8,128)(2,1)S(1)} %reshape_squeeze.15), kind=kOutput, calls=%fused_computation.10 | convolution fusion | flops 2281963520 | bytes 21037056 | tf_op jit(solution)/shard_map/dot_general | solution.py:60
  551.2 1.7 copy.19
  552.9 0.0 copy-done.2
  552.9 1.0 fusion.15
  553.9 72.5 %all-reduce = (f32[]{:T(128)}, f32[]{:T(128)}) all-reduce(f32[]{:T(128)} %get-tuple-element.4, f32[]{:T(128)} %get-tuple-element.3), channel_id=1, replica_groups=mesh['row'=16,'col'=8] {'row','col'}, use_global_device_ids=true, to_apply=%region_1.0 | all-reduce | flops 2 | bytes 16 | tf_op jit(solution)/shard_map/psum | solution.py:78
  627.7 1.3 fusion.17
  629.0 0.0 copy-done.1
  (1 shorter events, 0.0 us)
Async XLA Ops:
  0.6 60.8 %copy-start = (bf16[34,34,4,4]{1,3,2,0:T(4,128)(2,1)S(1)}, bf16[34,34,4,4]{1,3,2,0:T(4,128)(2,1)}, u32[]{:S(2)}) copy-start(bf16[34,34,4,4]{1,3,2,0:T(4,128)(2,1)} %param.12) | copy-start | bytes 110980
  3.8 10.7 %collective-permute-start = (bf16[128,16,128]{2,1,0:T(8,128)(2,1)S(1)}, bf16[128,16,128]{2,1,0:T(8,128)(2,1)S(1)}, u32[]{:S(2)}, u32[]{:S(2)}) collective-permute-start(bf16[128,16,128]{2,1,0:T(8,128)(2,1)S(1)} %broadcast_multiply_fusion), channel_id=1, source_target_pairs={{0,1},{1,2},{2,3},{3,4},{4,5},{5,6},{6,7},{8,9},{9,10},{10,11},{11... | collective-permute-start | bytes 1572872 | tf_op jit(solution)/shard_map/ppermute | solution.py:12
  8.4 10.5 %collective-permute-start.1 = (bf16[128,16,128]{2,1,0:T(8,128)(2,1)S(1)}, bf16[128,16,128]{2,1,0:T(8,128)(2,1)S(1)}, u32[]{:S(2)}, u32[]{:S(2)}) collective-permute-start(bf16[128,16,128]{2,1,0:T(8,128)(2,1)S(1)} %broadcast_multiply_fusion), channel_id=1, source_target_pairs={{1,0},{2,1},{3,2},{4,3},{5,4},{6,5},{7,6},{9,8},{10,9},{11,10},{12... | collective-permute-start | bytes 1572872 | tf_op jit(solution)/shard_map/ppermute | solution.py:15
  61.4 21.4 %copy-start.4 = (bf16[34,34,4,4]{1,3,2,0:T(4,128)(2,1)S(1)}, bf16[34,34,4,4]{1,3,2,0:T(4,128)(2,1)}, u32[]{:S(2)}) copy-start(bf16[34,34,4,4]{1,3,2,0:T(4,128)(2,1)} %param.11) | copy-start | bytes 110980
  151.0 380.1 %collective-permute-start.2 = (bf16[4352,2048]{1,0:T(8,128)(2,1)}, bf16[4352,2048]{1,0:T(8,128)(2,1)}, u32[]{:S(2)}, u32[]{:S(2)}) collective-permute-start(bf16[4352,2048]{1,0:T(8,128)(2,1)} %reshape.84), channel_id=1, source_target_pairs={{0,8},{8,16},{16,24},{24,32},{32,40},{40,48},{48,56},{56,64},{64,7... | collective-permute-start | bytes 53477384 | tf_op jit(solution)/shard_map/ppermute | solution.py:23
  160.3 381.0 %collective-permute-start.3 = (bf16[4352,2048]{1,0:T(8,128)(2,1)}, bf16[4352,2048]{1,0:T(8,128)(2,1)}, u32[]{:S(2)}, u32[]{:S(2)}) collective-permute-start(bf16[4352,2048]{1,0:T(8,128)(2,1)} %reshape.84), channel_id=1, source_target_pairs={{8,0},{16,8},{24,16},{32,24},{40,32},{48,40},{56,48},{64,56},{72,6... | collective-permute-start | bytes 53477384 | tf_op jit(solution)/shard_map/ppermute | solution.py:23
  173.8 357.3 %copy-start.3 = (bf16[128,4352]{0,1:T(8,128)(2,1)S(1)}, bf16[128,4352]{0,1:T(8,128)(2,1)}, u32[]{:S(2)}) copy-start(bf16[128,4352]{0,1:T(8,128)(2,1)} %reshape_squeeze.14) | copy-start | bytes 3342340
  540.0 12.9 %copy-start.2 = (bf16[128,16,128]{2,1,0:T(8,128)(2,1)S(1)}, bf16[128,16,128]{2,1,0:T(8,128)(2,1)}, u32[]{:S(2)}) copy-start(bf16[128,16,128]{2,1,0:T(8,128)(2,1)} %param.8) | copy-start | bytes 1572868
  541.3 87.6 %copy-start.1 = (bf16[34,34,4,4]{1,3,2,0:T(4,128)(2,1)S(1)}, bf16[34,34,4,4]{1,3,2,0:T(4,128)(2,1)}, u32[]{:S(2)}) copy-start(bf16[34,34,4,4]{1,3,2,0:T(4,128)(2,1)} %param.12) | copy-start | bytes 110980
where the time goes:
time: 632 us; the launch traced here: 630 us
  waiting for transfers between devices  354 us (56%)
  local copies, waits for them, and re-layouts  94.7 us (15%)
  matrix products  82.9 us (13%)
  blocking collectives  72.5 us (11%)
  starting transfers between devices  17 us (3%)
    ppermute x2, waiting for transfers between devices, from_behind(): return lax.ppermute(block, axis, route)  350 us
    psum x1, blocking collectives, on_device(): lax.psum((jnp.sum(psi_float * applied), jnp.sum(psi_float * psi_float)),...  72.5 us
    reshape x1, local copies, waits for them, and re-layouts, on_device(): section_one.reshape(block_rows, site_states, site_states, mpo_width, bloc...  29.7 us
    reshape x1, local copies, waits for them, and re-layouts, on_device(): third_section.reshape(block_rows * mpo_width, states * block_rows)  29.3 us
    dot_general x3, matrix products, couple_left(): jnp.dot(coupling.reshape(block_rows, block_rows * mpo_width), operand, pr...  27.7 us
    dot_general x1, matrix products, on_device(): jnp.einsum('mnts,xasnb->xamtb', mpo_right, section_one, preferred_element...  21.4 us
    dot_general x1, matrix products, on_device(): jnp.einsum('dquo,woqzj->wduzj', first_site_operator, second_section, pref...  21.3 us
    convert_element_type x1, local copies, waits for them, and re-layouts, on_device(): third_section = jnp.einsum('dquo,woqzj->wduzj', first_site_operator, seco...  17.6 us
  transfers between devices with their start and end apart: 4, of which 3 were waited for; matrix products, arithmetic and copies ran while one was open for 5% of the time, Pallas kernels for 0%

commit v1 on v0

--- a/solution.py
+++ b/solution.py
@@ -34,11 +34,13 @@
 def on_device(
     psi, env_left, env_right, first_site_operator, mpo_right, block_mask, left_live, right_live
 ):
-    blocks = env_left.shape[0]
     block_rows = env_left.shape[2]
     mpo_width = env_left.shape[4]
     states = psi.shape[1]
     site_states = first_site_operator.shape[2]
+    couplings = env_left[0].reshape(3, block_rows, block_rows * mpo_width)
+    from_next_row = from_behind(couplings[0], "row", -1)
+    from_prev_row = from_behind(couplings[2], "row", 1)
     live_mask = live_pattern(block_mask, left_live, right_live, block_rows)
     masked_wavefunction = psi * live_mask[:, None, :].astype(jnp.bfloat16)
     widened = padded(masked_wavefunction, (("col", 2),), block_rows)
@@ -54,24 +56,18 @@
     third_section = jnp.einsum(
         "dquo,woqzj->wduzj", first_site_operator, second_section, preferred_element_type=jnp.float32
     ).astype(jnp.bfloat16)
-    outcomes = [third_section.reshape(block_rows * mpo_width, states * block_rows)]
+    outcome = third_section.reshape(block_rows * mpo_width, states * block_rows)
 
     def couple_left(coupling, operand):
-        return jnp.dot(
-            coupling.reshape(block_rows, block_rows * mpo_width),
-            operand,
-            preferred_element_type=jnp.float32,
-        )
+        return jnp.dot(coupling, operand, preferred_element_type=jnp.float32)
 
-    running = couple_left(env_left[0, 1], outcomes[0])
-    totals = [running]
-    from_prev = from_behind(outcomes[blocks - 1], "row", 1)
-    from_next = from_behind(outcomes[0], "row", -1)
-    totals[0] = totals[0] + couple_left(env_left[0, 0], from_prev)
-    totals[blocks - 1] = totals[blocks - 1] + couple_left(env_left[blocks - 1, 2], from_next)
-    hamiltonian_times_wavefunction = jnp.stack(totals).reshape(
-        blocks * block_rows, states, block_rows
-    )
+    to_next = couple_left(from_next_row, outcome)
+    to_prev = couple_left(from_prev_row, outcome)
+    from_prev = from_behind(to_next, "row", 1)
+    from_next = from_behind(to_prev, "row", -1)
+    own = couple_left(couplings[1], outcome)
+    total = own + from_prev + from_next
+    hamiltonian_times_wavefunction = total.reshape(block_rows, states, block_rows)
     live_float = live_mask[:, None, :].astype(jnp.float32)
     applied = hamiltonian_times_wavefunction * live_float
     psi_float = masked_wavefunction.astype(jnp.float32)

time: 632 us -> 291 us (0.46)
  waiting for transfers between devices: 354 us -> 20.4 us
    ppermute x2 -> x4, waiting for transfers between devices: 350 us -> 20.4 us  [from_behind(): return lax.ppermute(block, axis, route)]
    dot_general x3, matrix products: 27.7 us -> 20.6 us  [couple_left(): return jnp.dot(coupling, operand, preferred_element_type=jnp.float32)]
    reshape x1 -> x2, local copies, waits for them, and re-layouts: 29.3 us -> 29.9 us  [the longest x1 29.4 us: on_device(): outcome = third_section.reshape(block_rows * mpo_width, states * block_rows)]
  transfers between devices with their start and end apart: 4 -> 6, of which waited for: 3 -> 2; matrix products, arithmetic and copies ran while one was open for 5% -> 60% of each run, Pallas kernels for 0% -> 0%
where the time goes in v1:
time: 291 us; the launch traced here: 289 us
  local copies, waits for them, and re-layouts  95.4 us (33%)
  matrix products  77.7 us (27%)
  blocking collectives  68.5 us (24%)
  waiting for transfers between devices  20.4 us (7%)
  starting transfers between devices  16.8 us (6%)
  between operations  5.23 us (2%)
  other arithmetic  5.12 us (2%)
    psum x1, blocking collectives, on_device(): lax.psum((jnp.sum(psi_float * applied), jnp.sum(psi_float * psi_float)),...  68.5 us
    reshape x1, local copies, waits for them, and re-layouts, on_device(): section_one.reshape(block_rows, site_states, site_states, mpo_width, bloc...  29.7 us
    reshape x1, local copies, waits for them, and re-layouts, on_device(): outcome = third_section.reshape(block_rows * mpo_width, states * block_rows)  29.4 us
    dot_general x1, matrix products, on_device(): jnp.einsum('mnts,xasnb->xamtb', mpo_right, section_one, preferred_element...  21.4 us
    dot_general x1, matrix products, on_device(): jnp.einsum('dquo,woqzj->wduzj', first_site_operator, second_section, pref...  21.3 us
    dot_general x3, matrix products, couple_left(): return jnp.dot(coupling, operand, preferred_element_type=jnp.float32)  20.6 us
    ppermute x4, waiting for transfers between devices, from_behind(): return lax.ppermute(block, axis, route)  20.4 us
    convert_element_type x1, local copies, waits for them, and re-layouts, on_device(): third_section = jnp.einsum('dquo,woqzj->wduzj', first_site_operator, seco...  17.6 us
  transfers between devices with their start and end apart: 6, of which 2 were waited for; matrix products, arithmetic and copies ran while one was open for 60% of the time, Pallas kernels for 0%

profile of v1, /device:TPU:1, one launch (start us, length us, event | category | flops | bytes accessed | tf_op | source)
XLA Modules:
  0.0 289.1 jit_solution(1782736310769734725)
XLA Ops:
  0.6 0.0 copy-start
  2.6 0.1 and_convert_fusion
  2.7 1.1 broadcast_multiply_fusion
  3.8 4.6 %collective-permute-start = (bf16[128,16,128]{2,1,0:T(8,128)(2,1)S(1)}, bf16[128,16,128]{2,1,0:T(8,128)(2,1)}, u32[]{:S(2)}, u32[]{:S(2)}) collective-permute-start(bf16[128,16,128]{2,1,0:T(8,128)(2,1)S(1)} %broadcast_multiply_fusion), channel_id=1, source_target_pairs={{0,1},{1,2},{2,3},{3,4},{4,5},{5,6},{6,7},{8,9},{9,10},{10,11},{11... | collective-permute-start | bytes 1572872 | tf_op jit(solution)/shard_map/ppermute | solution.py:12
  8.4 1.9 collective-permute-start.1
  10.4 3.7 %fusion.21 = (bf16[1,1,128,128,34]{3,2,4,1,0:T(8,128)(2,1)}, bf16[1,1,128,128,34]{3,2,4,1,0:T(8,128)(2,1)S(1)}, bf16[1,1,128,128,34]{3,2,4,1,0:T(8,128)(2,1)}) fusion(bf16[1,3,128,128,34]{3,2,4,1,0:T(8,128)(2,1)} %param.9), kind=kLoop, calls=%fused_computation.30 | loop fusion | bytes 6684672 | tf_op jit(solution)/shard_map/slice | solution.py:42
  14.0 2.1 copy.17
  16.2 1.2 squeeze.10
  17.4 1.3 collective-permute-start.2
  18.7 2.1 copy.18
  20.9 1.2 squeeze.11
  22.0 5.0 %collective-permute-start.4 = (bf16[128,4352]{0,1:T(8,128)(2,1)}, bf16[128,4352]{0,1:T(8,128)(2,1)}, u32[]{:S(2)}, u32[]{:S(2)}) collective-permute-start(bf16[128,4352]{0,1:T(8,128)(2,1)} %squeeze.11), channel_id=1, source_target_pairs={{0,8},{8,16},{16,24},{24,32},{32,40},{40,48},{48,56},{56,64},{64,7... | collective-permute-start | bytes 3342344 | tf_op jit(solution)/shard_map/ppermute | solution.py:23
  27.0 6.0 %copy.13 = bf16[1,3,128,34,128]{4,3,2,1,0:T(8,128)(2,1)} copy(bf16[1,3,128,34,128]{4,2,3,1,0:T(8,128)(2,1)} %param.10) | data formatting | bytes 6684672 | tf_op args[2]
  33.1 1.4 copy.16
  34.5 0.4 squeeze.9
  34.9 0.0 collective-permute-done
  34.9 0.0 collective-permute-done.1
  34.9 1.5 pad_maximum_fusion
  36.4 14.5 %convolution_convert_fusion = bf16[2048,4352]{1,0:T(8,128)(2,1)} fusion(bf16[2048,384]{1,0:T(8,128)(2,1)S(1)} %bitcast.79, bf16[48,8,34,128]{3,2,1,0:T(8,128)(2,1)} %bitcast.78), kind=kOutput, calls=%fused_computation.7 | convolution fusion | flops 6854017024 | bytes 22740992 | tf_op jit(solution)/shard_map/dot_general | solution.py:49
  50.9 29.7 %reshape.95 = bf16[128,4,4,34,128,1]{4,3,2,1,0,5:T(8,128)(2,1)} reshape(bf16[2048,4352]{1,0:T(8,128)(2,1)} %convolution_convert_fusion) | data formatting | bytes 35651584 | tf_op jit(solution)/shard_map/reshape | solution.py:52
  80.6 0.0 copy-done
  80.6 0.0 copy-start.4
  80.6 21.4 %fusion.38 = bf16[128,4,34,4,128,1]{4,2,1,5,3,0:T(8,128)(2,1)} fusion(bf16[128,4,4,34,128,1]{4,3,2,1,0,5:T(8,128)(2,1)} %reshape.95, bf16[34,34,4,4,1,1]{1,3,2,0,4,5:T(4,128)(2,1)S(1)} %bitcast.76), kind=kOutput, calls=%fused_computation.2.clone.clone.clone.clone.1 | convolution fusion | flops 2433220608 | bytes 35688576 | tf_op jit(solution)/shard_map/mnts,xasnb->xamtb/dot_general | solution.py:53
  101.9 0.0 copy-done.4
  102.0 21.3 %fusion.3 = bf16[128,34,4,4,128]{4,1,2,3,0:T(8,128)(2,1)} fusion(bf16[34,34,4,4,1,1]{1,3,2,0,5,4:T(4,128)(2,1)S(1)} %bitcast.80, bf16[128,4,34,4,128,1]{4,2,1,5,3,0:T(8,128)(2,1)} %fusion.38), kind=kOutput, calls=%fused_computation.4 | convolution fusion | flops 2433220608 | bytes 35688576 | tf_op jit(solution)/shard_map/dquo,woqzj->wduzj/dot_general | solution.py:56
  123.2 17.6 %copy.15 = bf16[128,34,4,4,128]{4,3,2,1,0:T(4,128)(2,1)} copy(bf16[128,34,4,4,128]{4,1,2,3,0:T(8,128)(2,1)} %fusion.3) | data formatting | bytes 35651584 | tf_op jit(solution)/shard_map/convert_element_type | solution.py:58
  140.9 29.4 %reshape.93 = bf16[4352,2048]{1,0:T(8,128)(2,1)} reshape(bf16[128,34,4,4,128]{4,3,2,1,0:T(4,128)(2,1)} %copy.15) | data formatting | bytes 35651584 | tf_op jit(solution)/shard_map/reshape | solution.py:59
  170.2 0.0 copy-start.2
  170.2 0.0 collective-permute-done.2
  170.2 9.3 %convolution_bitcast_fusion.1 = f32[128,2048]{0,1:T(8,128)S(1)} fusion(bf16[4352,2048]{1,0:T(8,128)(2,1)} %reshape.93, bf16[128,4352]{0,1:T(8,128)(2,1)} %collective-permute-done.2), kind=kOutput, calls=%fused_computation.11 | convolution fusion | flops 2281701376 | bytes 19988480 | tf_op jit(solution)/shard_map/dot_general | solution.py:62
  179.5 2.4 collective-permute-start.3
  182.0 0.0 collective-permute-done.4
  182.0 0.0 copy-done.2
  182.0 6.3 %convolution_bitcast_fusion = f32[128,2048]{0,1:T(8,128)S(1)} fusion(bf16[4352,2048]{1,0:T(8,128)(2,1)S(1)} %copy-done.2, bf16[128,4352]{0,1:T(8,128)(2,1)} %collective-permute-done.4), kind=kOutput, calls=%fused_computation.10 | convolution fusion | flops 2281701376 | bytes 19988480 | tf_op jit(solution)/shard_map/dot_general | solution.py:62
  188.3 1.6 collective-permute-start.5
  189.8 5.0 %convolution_bitcast_fusion.2 = f32[128,2048]{0,1:T(8,128)S(1)} fusion(bf16[4352,2048]{1,0:T(8,128)(2,1)S(1)} %copy-done.2, bf16[128,4352]{0,1:T(8,128)(2,1)S(1)} %squeeze.9), kind=kOutput, calls=%fused_computation.12 | convolution fusion | flops 2281701376 | bytes 19988480 | tf_op jit(solution)/shard_map/dot_general | solution.py:62
  194.9 0.0 copy-start.3
  194.9 9.8 %collective-permute-done.3 = f32[128,2048]{0,1:T(8,128)S(1)} collective-permute-done((f32[128,2048]{0,1:T(8,128)S(1)}, f32[128,2048]{0,1:T(8,128)S(1)}, u32[]{:S(2)}, u32[]{:S(2)}) %collective-permute-start.3) | collective-permute-done | bytes 1048608 | tf_op jit(solution)/shard_map/ppermute | solution.py:23
  204.7 10.5 %collective-permute-done.5 = f32[128,2048]{0,1:T(8,128)S(1)} collective-permute-done((f32[128,2048]{0,1:T(8,128)S(1)}, f32[128,2048]{0,1:T(8,128)S(1)}, u32[]{:S(2)}, u32[]{:S(2)}) %collective-permute-start.5) | collective-permute-done | bytes 1048608 | tf_op jit(solution)/shard_map/ppermute | solution.py:23
  215.2 0.2 add_add_fusion
  215.4 0.0 copy-start.1
  215.4 0.5 copy.19
  215.9 0.0 copy-done.3
  215.9 1.0 fusion.15
  216.9 68.5 %all-reduce = (f32[]{:T(128)}, f32[]{:T(128)}) all-reduce(f32[]{:T(128)} %get-tuple-element.4, f32[]{:T(128)} %get-tuple-element.3), channel_id=1, replica_groups=mesh['row'=16,'col'=8] {'row','col'}, use_global_device_ids=true, to_apply=%region_1.0 | all-reduce | flops 2 | bytes 16 | tf_op jit(solution)/shard_map/psum | solution.py:74
  286.7 1.3 fusion.17
  287.9 0.0 copy-done.1
  (1 shorter events, 0.0 us)
Async XLA Ops:
  0.6 80.0 %copy-start = (bf16[34,34,4,4]{1,3,2,0:T(4,128)(2,1)S(1)}, bf16[34,34,4,4]{1,3,2,0:T(4,128)(2,1)}, u32[]{:S(2)}) copy-start(bf16[34,34,4,4]{1,3,2,0:T(4,128)(2,1)} %param.12) | copy-start | bytes 110980
  3.8 31.0 %collective-permute-start = (bf16[128,16,128]{2,1,0:T(8,128)(2,1)S(1)}, bf16[128,16,128]{2,1,0:T(8,128)(2,1)}, u32[]{:S(2)}, u32[]{:S(2)}) collective-permute-start(bf16[128,16,128]{2,1,0:T(8,128)(2,1)S(1)} %broadcast_multiply_fusion), channel_id=1, source_target_pairs={{0,1},{1,2},{2,3},{3,4},{4,5},{5,6},{6,7},{8,9},{9,10},{10,11},{11... | collective-permute-start | bytes 1572872 | tf_op jit(solution)/shard_map/ppermute | solution.py:12
  8.4 26.4 %collective-permute-start.1 = (bf16[128,16,128]{2,1,0:T(8,128)(2,1)S(1)}, bf16[128,16,128]{2,1,0:T(8,128)(2,1)}, u32[]{:S(2)}, u32[]{:S(2)}) collective-permute-start(bf16[128,16,128]{2,1,0:T(8,128)(2,1)S(1)} %broadcast_multiply_fusion), channel_id=1, source_target_pairs={{1,0},{2,1},{3,2},{4,3},{5,4},{6,5},{7,6},{9,8},{10,9},{11,10},{12... | collective-permute-start | bytes 1572872 | tf_op jit(solution)/shard_map/ppermute | solution.py:15
  17.4 152.8 %collective-permute-start.2 = (bf16[128,4352]{0,1:T(8,128)(2,1)}, bf16[128,4352]{0,1:T(8,128)(2,1)}, u32[]{:S(2)}, u32[]{:S(2)}) collective-permute-start(bf16[128,4352]{0,1:T(8,128)(2,1)} %squeeze.10), channel_id=1, source_target_pairs={{8,0},{16,8},{24,16},{32,24},{40,32},{48,40},{56,48},{64,56},{72,6... | collective-permute-start | bytes 3342344 | tf_op jit(solution)/shard_map/ppermute | solution.py:23
  22.0 159.9 %collective-permute-start.4 = (bf16[128,4352]{0,1:T(8,128)(2,1)}, bf16[128,4352]{0,1:T(8,128)(2,1)}, u32[]{:S(2)}, u32[]{:S(2)}) collective-permute-start(bf16[128,4352]{0,1:T(8,128)(2,1)} %squeeze.11), channel_id=1, source_target_pairs={{0,8},{8,16},{16,24},{24,32},{32,40},{40,48},{48,56},{56,64},{64,7... | collective-permute-start | bytes 3342344 | tf_op jit(solution)/shard_map/ppermute | solution.py:23
  80.6 21.4 %copy-start.4 = (bf16[34,34,4,4]{1,3,2,0:T(4,128)(2,1)S(1)}, bf16[34,34,4,4]{1,3,2,0:T(4,128)(2,1)}, u32[]{:S(2)}) copy-start(bf16[34,34,4,4]{1,3,2,0:T(4,128)(2,1)} %param.11) | copy-start | bytes 110980
  170.2 11.7 %copy-start.2 = (bf16[4352,2048]{1,0:T(8,128)(2,1)S(1)}, bf16[4352,2048]{1,0:T(8,128)(2,1)}, u32[]{:S(2)}) copy-start(bf16[4352,2048]{1,0:T(8,128)(2,1)} %reshape.93) | copy-start | bytes 53477380
  179.5 25.2 %collective-permute-start.3 = (f32[128,2048]{0,1:T(8,128)S(1)}, f32[128,2048]{0,1:T(8,128)S(1)}, u32[]{:S(2)}, u32[]{:S(2)}) collective-permute-start(f32[128,2048]{0,1:T(8,128)S(1)} %convolution_bitcast_fusion.1), channel_id=1, source_target_pairs={{0,8},{8,16},{16,24},{24,32},{32,40},{40,48},{48,56},{56,64},{64,7... | collective-permute-start | bytes 3145736 | tf_op jit(solution)/shard_map/ppermute | solution.py:23
  188.3 27.0 %collective-permute-start.5 = (f32[128,2048]{0,1:T(8,128)S(1)}, f32[128,2048]{0,1:T(8,128)S(1)}, u32[]{:S(2)}, u32[]{:S(2)}) collective-permute-start(f32[128,2048]{0,1:T(8,128)S(1)} %convolution_bitcast_fusion), channel_id=1, source_target_pairs={{8,0},{16,8},{24,16},{32,24},{40,32},{48,40},{56,48},{64,56},{72,6... | collective-permute-start | bytes 3145736 | tf_op jit(solution)/shard_map/ppermute | solution.py:23
  194.9 21.1 %copy-start.3 = (bf16[128,16,128]{2,1,0:T(8,128)(2,1)S(1)}, bf16[128,16,128]{2,1,0:T(8,128)(2,1)}, u32[]{:S(2)}) copy-start(bf16[128,16,128]{2,1,0:T(8,128)(2,1)} %param.8) | copy-start | bytes 1572868
  215.4 72.6 %copy-start.1 = (bf16[34,34,4,4]{1,3,2,0:T(4,128)(2,1)S(1)}, bf16[34,34,4,4]{1,3,2,0:T(4,128)(2,1)}, u32[]{:S(2)}) copy-start(bf16[34,34,4,4]{1,3,2,0:T(4,128)(2,1)} %param.12) | copy-start | bytes 110980
